TPU v7x, 128 devices: a whole 4x4x4 slice. The times are simulated.
128 devices in a mesh: req: 64 (over z, y, x), col: 2 (over core).
Axes of the slice: x: 4, y: 4, z: 4, core: 2. Of those that a mesh axis runs over, the one named last changes fastest.
Arguments:
- tokens: bfloat16 [32768, 1024], P(('req', 'col')), may hold values from -6 to 6
- norm_gain_pair: float32 [2, 1024], replicated, may hold values from 0.5 to 1.5
- query_key_value_weight: bfloat16 [3, 1024, 1024], P(None, None, 'col'), may hold values from -1 to 1
- head_gate_weight: bfloat16 [2, 1024, 8], P(None, None, 'col'), may hold values from -0.1875 to 0.1875
- decay_logit_bias: float32 [8], P('col'), may hold values from -1 to 1024, as said below
- adapter_down_factor: bfloat16 [64, 1024, 16], P('col'), may hold values from -0.1875 to 0.1875
- adapter_up_factor: bfloat16 [64, 16, 1024], P(None, None, 'col'), may hold values from -1.5 to 1.5
- lengths: int32 [64, 2, 3], P('req'), may hold values from 1 to 128, 256 in all within a row
- request_adapter_index: int32 [64, 6], P('req'), may hold values from 0 to 63
- request_cache_index: int32 [64, 6], P('req'), may hold values from 0 to 511
- caches: bfloat16 [256, 8, 128, 128], P('req', 'col'), may hold values from -6 to 6
- head_output_weight: bfloat16 [1024, 1024], P('col'), may hold values from -0.1875 to 0.1875
- feedforward_weight: bfloat16 [3, 1024, 2816], P(None, None, 'col'), may hold values from -0.1875 to 0.1875
Outputs:
- layer_out: bfloat16 [32768, 1024], P(('req', 'col'))
Inputs may be any that keep to these rules, and one draw needn't show every extreme that they name: The 3 lengths of one device sum to 256, and the longest of them is exactly 128. `request_cache_index`: a value of 256 or more means that the request has no cached memory state. `decay_logit_bias`: at most the logarithm of 512.
All inputs are finite; a program needn't handle non-finite values.
Results may differ from a plain program's by a relative error of at most 0.015.
Values may be sent and summed in bfloat16 or wider, within the bound.
No kernel may reach another device: no remote copies, remote signals or barrier semaphores. Data moves between devices by JAX's collectives and lax.ppermute only.
A program may use at most 192 MiB of HBM per device.

v0:
```python
import math
import jax
import jax.numpy as jnp
from jax import lax
from jax.sharding import PartitionSpec as P

epsilon = 1e-05


def rms_scale(values, gain):
    widened = values.astype(jnp.float32)
    factor = lax.rsqrt(jnp.mean(widened * widened, axis=-1, keepdims=True) + epsilon)
    return (widened * factor * gain).astype(jnp.bfloat16)


def on_device(
    tokens,
    norm_gain_pair,
    query_key_value_weight,
    head_gate_weight,
    decay_logit_bias,
    adapter_down_factor,
    adapter_up_factor,
    lengths,
    request_adapter_index,
    request_cache_index,
    caches,
    head_output_weight,
    feedforward_weight,
):
    tok_rows, width = tokens.shape
    col_count = lax.axis_size("col")
    group = tok_rows * col_count
    head_cols = query_key_value_weight.shape[2]
    local_heads = head_gate_weight.shape[2]
    head_size = head_cols // local_heads
    group_lengths = lengths[0].reshape(-1)
    scale = 1.0 / math.sqrt(head_size)
    normalized_rows = rms_scale(tokens, norm_gain_pair[0])
    gathered = lax.all_gather(normalized_rows, "col", axis=0, tiled=True)
    positions = jnp.arange(group, dtype=jnp.int32)
    ends = jnp.cumsum(group_lengths)
    starts = ends - group_lengths
    member = (
        (positions[:, None] >= starts[None, :]) & (positions[:, None] < ends[None, :])
    ).astype(jnp.float32)
    segment = jnp.sum((positions[:, None] >= ends[None, :]).astype(jnp.int32), axis=1)
    projected = jnp.einsum(
        "td,kdc->ktc", gathered, query_key_value_weight, preferred_element_type=jnp.float32
    )
    token_segment = lax.all_gather(adapter_down_factor, "col", axis=0, tiled=True)
    numbers = jnp.arange(token_segment.shape[0], dtype=jnp.int32)
    select = (request_adapter_index[0][:, None] == numbers[None, :]).astype(jnp.bfloat16)
    chosen = jnp.einsum(
        "sa,adr->sdr", select, token_segment, preferred_element_type=jnp.float32
    ).astype(jnp.bfloat16)
    per_request = jnp.einsum("td,sdr->tsr", gathered, chosen, preferred_element_type=jnp.float32)
    low_rank_delta = jnp.sum(member[:, :, None] * per_request, axis=1)
    low_rank_delta = low_rank_delta.astype(jnp.bfloat16)
    adapter_onehot = (
        request_adapter_index[0][:, None]
        == jnp.arange(adapter_up_factor.shape[0], dtype=jnp.int32)[None, :]
    ).astype(jnp.bfloat16)
    up_chosen = jnp.einsum(
        "gq,qjl->gjl", adapter_onehot, adapter_up_factor, preferred_element_type=jnp.float32
    ).astype(jnp.bfloat16)
    delta_all = jnp.einsum(
        "tr,src->tsc", low_rank_delta, up_chosen, preferred_element_type=jnp.float32
    )
    delta = jnp.sum(member[:, :, None] * delta_all, axis=1)
    queries = (projected[0] + delta).astype(jnp.bfloat16).reshape(group, local_heads, head_size)
    keys = projected[1].astype(jnp.bfloat16).reshape(group, local_heads, head_size)
    values = projected[2].astype(jnp.bfloat16).reshape(group, local_heads, head_size)
    gate_terms = jnp.einsum(
        "td,kdh->kth", gathered, head_gate_weight, preferred_element_type=jnp.float32
    )
    log_keep = jax.nn.log_sigmoid(gate_terms[0] + decay_logit_bias[None, :])
    mix_gate = jax.nn.sigmoid(gate_terms[1])
    running = jnp.cumsum(log_keep, axis=0)
    before = running - log_keep
    start_hot = (positions[None, :] == starts[:, None]).astype(jnp.float32)
    start_level = jnp.sum(start_hot[:, :, None] * before[None, :, :], axis=1)
    level = running - jnp.sum(member[:, :, None] * start_level[None, :, :], axis=1)
    token_segment = lax.all_gather(caches, "req", axis=0, tiled=True)
    numbers = jnp.arange(token_segment.shape[0], dtype=jnp.int32)
    select = (request_cache_index[0][:, None] == numbers[None, :]).astype(jnp.bfloat16)
    states = jnp.einsum(
        "sn,nhij->shij", select, token_segment, preferred_element_type=jnp.float32
    ).astype(jnp.bfloat16)
    from_state = jnp.einsum("thi,shij->tshj", queries, states, preferred_element_type=jnp.float32)
    carried = jnp.sum(member[:, :, None, None] * from_state, axis=1) * jnp.exp(level)[:, :, None]
    block = min(512, group)

    def one_block(index):
        begin = index * block
        scores = (
            jnp.einsum("qhd,khd->hqk", queries, keys, preferred_element_type=jnp.float32) * scale
        )
        q_pos = begin + jnp.arange(block, dtype=jnp.int32)
        allowed = (segment[:, None] == segment[None, :]) & (positions[None, :] <= q_pos[:, None])
        masked = jnp.where(allowed[None], scores, -jnp.inf)
        peak = jnp.max(masked, axis=2, keepdims=True)
        weights = jnp.exp(masked - peak)
        probs = (weights / jnp.sum(weights, axis=2, keepdims=True)).astype(jnp.bfloat16)
        attended = jnp.einsum("hqk,khd->qhd", probs, values, preferred_element_type=jnp.float32)
        gap = jnp.where(allowed[None], running.T[:, :, None] - running.T[:, None, :], -jnp.inf)
        memory_w = (scores * jnp.exp(gap)).astype(jnp.bfloat16)
        recalled = jnp.einsum("hqk,khd->qhd", memory_w, values, preferred_element_type=jnp.float32)
        recalled = recalled + carried
        factor = lax.rsqrt(jnp.mean(recalled * recalled, axis=2, keepdims=True) + epsilon)
        combined = attended + mix_gate[:, :, None] * recalled * factor
        return combined.astype(jnp.bfloat16).reshape(block, head_cols)

    blocks = lax.map(one_block, jnp.arange(group // block, dtype=jnp.int32))
    head_out = blocks.reshape(group, head_cols)
    attn_proj = lax.psum_scatter(
        jnp.dot(head_out, head_output_weight, preferred_element_type=jnp.float32),
        "col",
        scatter_dimension=0,
        tiled=True,
    )
    mixed = (tokens.astype(jnp.float32) + attn_proj).astype(jnp.bfloat16)
    normed_two = rms_scale(mixed, norm_gain_pair[1])
    token_segment = lax.all_gather(feedforward_weight, "col", axis=2, tiled=True)
    gate_up = jnp.einsum(
        "td,kdf->ktf", normed_two, token_segment[:2], preferred_element_type=jnp.float32
    )
    hidden = (jax.nn.silu(gate_up[0]) * gate_up[1]).astype(jnp.bfloat16)
    feed = jnp.einsum("tf,df->td", hidden, token_segment[2], preferred_element_type=jnp.float32)
    return (mixed.astype(jnp.float32) + feed).astype(jnp.bfloat16)


def solution(mesh):
    placed = (
        P(("req", "col"), None),
        P(),
        P(None, None, "col"),
        P(None, None, "col"),
        P("col"),
        P("col", None, None),
        P(None, None, "col"),
        P("req", None, None),
        P("req", None),
        P("req", None),
        P("req", "col", None, None),
        P("col", None),
        P(None, None, "col"),
    )
    return jax.shard_map(
        on_device, mesh=mesh, in_specs=placed, out_specs=P(("req", "col"), None), check_vma=False
    )
```

profile of v0, /device:TPU:1, one launch (start us, length us, event | category | flops | bytes accessed | tf_op | source)
XLA Modules:
  0.0 319.6 jit_solution(7090761878730281534)
XLA Ops:
  6.5 1.4 fusion.38
  7.9 1.4 fusion.87
  9.3 2.0 fusion.40
  15.6 2.4 convolution_convert_fusion
  18.1 8.8 %all-gather.5.cloned.1.call-done = bf16[512,1024]{1,0:T(8,128)(2,1)} async-done(((bf16[256,1024]{1,0:T(8,128)(2,1)}), bf16[512,1024]{1,0:T(8,128)(2,1)}) %all-gather.5.cloned.1.call-update) | async-done | bytes 1048592 | tf_op jit(solution)/shard_map/all_gather | solution.py:40
  26.9 1.6 convolution_bitcast_fusion.1
  29.1 1.3 fusion.84
  31.7 3.0 reduce-window.18
  34.8 1.4 slice_reduce_fusion
  36.2 1.3 reduce-window.19
  38.9 3.2 %fusion.88 = (bf16[3,512,512]{1,2,0:T(8,128)(2,1)S(1)}, f32[3,512,512]{1,2,0:T(8,128)S(1)}) fusion(bf16[3,1024,512]{2,1,0:T(8,128)(2,1)S(1)} %copy-done, bf16[512,1024]{1,0:T(8,128)(2,1)} %all-gather.5.cloned.1.call-done), kind=kOutput, calls=%fused_computation.113 | convolution fusion | flops 1611399168 | bytes 8912896 | tf_op jit(solution)/shard_map/td,kdc->ktc/dot_general | solution.py:48
  44.8 3.9 %fusion.35 = bf16[6,1024,16]{1,0,2:T(8,128)(2,1)S(1)} fusion(bf16[64,1024,16]{1,2,0:T(8,128)(2,1)} %all-gather.7.cloned.1.call-done, s32[6]{0:T(128)S(1)} %bitcast.135), kind=kOutput, calls=%fused_computation.41 | convolution fusion | flops 12681600 | bytes 2293784 | tf_op jit(solution)/shard_map/sa,adr->sdr/dot_general | solution.py:54
  50.9 4.8 %fusion.89 = (f32[4,512]{1,0:T(4,128)S(1)}, f32[4,512,512]{1,2,0:T(8,128)}) fusion(pred[512,512]{0,1:T(8,128)(4,1)S(1)} %fusion.48, bf16[512,4,128]{0,2,1:T(8,128)(2,1)S(1)} %add_convert_fusion, bf16[512,4,128]{0,2,1:T(8,128)(2,1)} %bitcast.128), kind=kOutput, calls=%fused_computation.114 | convolution fusion | flops 272630272 | bytes 5513216 | tf_op jit(solution)/shard_map/while/body/eval_jaxpr/sub | solution.py:103
  55.7 152.0 %all-gather.9.cloned.1.call-done = bf16[256,4,128,128]{3,2,1,0:T(8,128)(2,1)} async-done(((bf16[4,4,128,128]{3,2,1,0:T(8,128)(2,1)}), bf16[256,4,128,128]{3,2,1,0:T(8,128)(2,1)}) %all-gather.9.cloned.1.call-update) | async-done | bytes 33554448 | tf_op jit(solution)/shard_map/all_gather | solution.py:84
  207.7 32.0 %fusion.20 = bf16[6,4,128,128]{3,0,2,1:T(8,128)(2,1)S(1)} fusion(bf16[256,4,128,128]{3,2,1,0:T(8,128)(2,1)} %all-gather.9.cloned.1.call-done, s32[6]{0:T(128)S(1)} %bitcast.138), kind=kOutput, calls=%fused_computation.33 | convolution fusion | flops 201721344 | bytes 34340888 | tf_op jit(solution)/shard_map/sn,nhij->shij/dot_general | solution.py:87
  239.8 2.0 fusion.5
  241.9 4.1 %multiply_reduce_fusion.1 = (f32[512,4]{0,1:T(4,128)S(1)}, f32[512,4,128]{0,2,1:T(8,128)}) fusion(f32[512,4,128]{0,2,1:T(8,128)} %fusion.5, f32[512,4]{0,1:T(4,128)S(1)} %copy-done.11, bf16[512,4,128]{0,2,1:T(8,128)(2,1)S(1)} %bitcast.126, f32[4,512]{1,0:T(4,128)S(1)} %bitcast.132, pred[512,512]{0,1:T(8,128)(4,1)S(1)} %fusion.48, ...), kind=kOutput, calls=%fused_computation.54 | convolution fusion | flops 543160320 | bytes 3956736 | tf_op jit(solution)/shard_map/while/body/eval_jaxpr/hqk,khd->qhd/dot_general | solution.py:108
  246.0 3.1 fusion.31
  249.1 2.1 fusion.93
  251.8 11.9 %reduce-scatter.2.cloned.1.call-done = f32[256,1024]{1,0:T(8,128)} async-done(((f32[512,1024]{1,0:T(8,128)}), f32[256,1024]{1,0:T(8,128)}) %reduce-scatter.2.cloned.1.call-update) | async-done | bytes 1048592 | tf_op jit(solution)/shard_map/reduce_scatter | solution.py:116
  263.7 1.5 fusion.42
  265.2 36.4 %all-gather.11.cloned.1.call-done = bf16[3,1024,2816]{2,1,0:T(8,128)(2,1)} async-done(((bf16[3,1024,1408]{2,1,0:T(8,128)(2,1)}), bf16[3,1024,2816]{2,1,0:T(8,128)(2,1)}) %all-gather.11.cloned.1.call-update) | async-done | bytes 17301520 | tf_op jit(solution)/shard_map/all_gather | solution.py:124
  301.6 6.1 %fusion.7 = f32[2,256,2816]{2,1,0:T(8,128)S(1)} fusion(bf16[3,1024,2816]{2,1,0:T(8,128)(2,1)} %all-gather.11.cloned.1.call-done, bf16[256,1024]{1,0:T(8,128)(2,1)S(1)} %get-tuple-element.24, f32[1024]{0:T(1024)S(1)} %bitcast.133, f32[256]{0:T(256)S(1)} %add_rsqrt_fusion.1), kind=kOutput, calls=%fused_computation.10 | convolution fusion | flops 2953838592 | bytes 17830912 | tf_op jit(solution)/shard_map/td,kdf->ktf/dot_general | solution.py:125
  307.7 5.4 %fusion.32 = bf16[256,1024]{1,0:T(8,128)(2,1)} fusion(bf16[3,1024,2816]{2,1,0:T(8,128)(2,1)} %all-gather.11.cloned.1.call-done, f32[2,256,2816]{2,1,0:T(8,128)S(1)} %fusion.7, bf16[256,1024]{1,0:T(8,128)(2,1)} %copy-done.7), kind=kOutput, calls=%fused_computation.40 | convolution fusion | flops 1481506816 | bytes 12582912 | tf_op jit(solution)/shard_map/tf,df->td/dot_general | solution.py:129
  (74 shorter events, 13.0 us)
Async XLA Ops:
  6.5 32.3 %copy-start = (bf16[3,1024,512]{2,1,0:T(8,128)(2,1)S(1)}, bf16[3,1024,512]{2,1,0:T(8,128)(2,1)}, u32[]{:S(2)}) copy-start(bf16[3,1024,512]{2,1,0:T(8,128)(2,1)} %param.15) | copy-start | bytes 9437188
  6.5 20.3 %all-gather.5.cloned.1.call-start = ((), (), s32[]{:S(2)}) async-start(), calls=%async_computation.1 | async-start | bytes 1572864 | tf_op jit(solution)/shard_map/all_gather | solution.py:40
  11.3 33.5 %all-gather.7.cloned.1.call-start = ((), (), s32[]{:S(2)}) async-start(), calls=%async_computation.2 | async-start | bytes 3145728 | tf_op jit(solution)/shard_map/all_gather | solution.py:51
  12.1 195.6 %all-gather.9.cloned.1.call-start = ((), (), s32[]{:S(2)}) async-start(), calls=%async_computation.3 | async-start | bytes 34078720 | tf_op jit(solution)/shard_map/all_gather | solution.py:84
  12.8 250.9 %reduce-scatter.2.cloned.1.call-start = ((), (), s32[]{:S(2)}) async-start(), calls=%async_computation.4 | async-start | bytes 3145728 | tf_op jit(solution)/shard_map/reduce_scatter | solution.py:116
  28.5 0.6 copy-start.8
  38.9 3.4 %copy-start.9 = (f32[2,512,4]{1,2,0:T(4,128)S(1)}, f32[2,512,4]{1,2,0:T(4,128)}, u32[]{:S(2)}) copy-start(f32[2,512,4]{1,2,0:T(4,128)} %copy-done.8) | copy-start | bytes 49156
  38.9 3.4 %copy-start.16 = (f32[4]{0:T(128)S(1)}, f32[4]{0:T(128)}, u32[]{:S(2)}) copy-start(f32[4]{0:T(128)} %param.17) | copy-start | bytes 52
  38.9 3.5 %copy-start.10 = (f32[6,512]{1,0:T(8,128)S(1)}, f32[6,512]{1,0:T(8,128)}, u32[]{:S(2)}) copy-start(f32[6,512]{1,0:T(8,128)} %fusion.62) | copy-start | bytes 36868
  42.1 2.7 copy-start.15
  42.1 6.7 %copy-start.3 = (bf16[512,1024]{1,0:T(8,128)(2,1)S(1)}, bf16[512,1024]{1,0:T(8,128)(2,1)}, u32[]{:S(2)}) copy-start(bf16[512,1024]{1,0:T(8,128)(2,1)} %all-gather.5.cloned.1.call-done) | copy-start | bytes 3145732
  50.9 156.8 %copy-start.17 = (s32[1,6]{1,0:T(1,128)S(1)}, s32[1,6]{1,0:T(1,128)}, u32[]{:S(2)}) copy-start(s32[1,6]{1,0:T(1,128)} %param.22) | copy-start | bytes 76
  239.8 2.1 copy-start.5
  239.8 2.1 copy-start.6
  239.8 2.0 copy-start.11
  239.8 2.0 copy-start.12
  241.9 4.1 %copy-start.13 = (f32[512,4]{0,1:T(4,128)S(1)}, f32[512,4]{0,1:T(4,128)}, u32[]{:S(2)}) copy-start(f32[512,4]{0,1:T(4,128)} %fusion.69) | copy-start | bytes 24580
  246.0 3.1 copy-start.4
  251.2 12.5 %copy-start.2 = (bf16[256,1024]{1,0:T(8,128)(2,1)S(1)}, bf16[256,1024]{1,0:T(8,128)(2,1)}, u32[]{:S(2)}) copy-start(bf16[256,1024]{1,0:T(8,128)(2,1)} %param.13) | copy-start | bytes 1572868
  251.2 50.4 %copy-start.14 = (f32[1,1024]{1,0:T(1,128)S(1)}, f32[1,1024]{1,0:T(1,128)}, u32[]{:S(2)}) copy-start(f32[1,1024]{1,0:T(1,128)} %get-tuple-element.27) | copy-start | bytes 12292
  251.2 50.4 %all-gather.11.cloned.1.call-start = ((), (), s32[]{:S(2)}) async-start(), calls=%async_computation.5 | async-start | bytes 25952256 | tf_op jit(solution)/shard_map/all_gather | solution.py:124
  265.1 36.5 %copy-start.7 = (bf16[256,1024]{1,0:T(8,128)(2,1)}, bf16[256,1024]{1,0:T(8,128)(2,1)S(1)}, u32[]{:S(2)}) copy-start(bf16[256,1024]{1,0:T(8,128)(2,1)S(1)} %get-tuple-element.24) | copy-start | bytes 1572868
  307.7 5.4 %copy-start.1 = (bf16[3,1024,512]{2,1,0:T(8,128)(2,1)S(1)}, bf16[3,1024,512]{2,1,0:T(8,128)(2,1)}, u32[]{:S(2)}) copy-start(bf16[3,1024,512]{2,1,0:T(8,128)(2,1)} %param.15) | copy-start | bytes 9437188
Sparse Core Ops, SparseCore 0:
  11.5 15.3 all-gather.4
  28.5 14.6 all-gather.6
  46.0 161.6 all-gather.8
  251.3 12.3 reduce-scatter.1
  265.3 36.2 all-gather.10
where the time goes:
time: 320 us
  waiting for transfers between devices  211 us (66%)
  matrix products  72.2 us (23%)
  other arithmetic  14.3 us (4%)
  between operations  13.4 us (4%)
  local copies, waits for them, and re-layouts  8.44 us (3%)
    all_gather x1, waiting for transfers between devices, on_device(): token_segment = lax.all_gather(caches, 'req', axis=0, tiled=True)  152 us
    all_gather x1, waiting for transfers between devices, on_device(): lax.all_gather(feedforward_weight, 'col', axis=2, tiled=True)  36.4 us
    dot_general x1, matrix products, on_device(): jnp.einsum('sn,nhij->shij', select, token_segment, preferred_element_type...  32 us
    reduce_scatter x1, waiting for transfers between devices, on_device(): lax.psum_scatter(jnp.dot(head_out, head_output_weight, preferred_element_...  11.9 us
    all_gather x1, waiting for transfers between devices, on_device(): gathered = lax.all_gather(normalized_rows, 'col', axis=0, tiled=True)  8.81 us
  transfers between devices with their start and end apart: 5, of which 4 were waited for; matrix products, arithmetic and copies ran while one was open for 11% of the time, Pallas kernels for 0%

commit v1 on v0

--- a/solution.py
+++ b/solution.py
@@ -37,7 +37,8 @@
     group_lengths = lengths[0].reshape(-1)
     scale = 1.0 / math.sqrt(head_size)
     normalized_rows = rms_scale(tokens, norm_gain_pair[0])
-    gathered = lax.all_gather(normalized_rows, "col", axis=0, tiled=True)
+    repeated = jnp.stack([normalized_rows] * lax.axis_size("col"))
+    gathered = jnp.concatenate(lax.all_to_all(repeated, "col", 0, 0), axis=0)
     positions = jnp.arange(group, dtype=jnp.int32)
     ends = jnp.cumsum(group_lengths)
     starts = ends - group_lengths

time: 320 us -> 303 us (0.947)
  waiting for transfers between devices: 211 us -> 196 us
  starting transfers between devices: 0.16 us -> 5.95 us
  other arithmetic: 14.3 us -> 8.95 us
  local copies, waits for them, and re-layouts: 8.44 us -> 3.95 us
    all_gather x1 -> x0, waiting for transfers between devices: 8.81 us -> none  [on_device(): gathered = lax.all_gather(normalized_rows, 'col', axis=0, tiled=True)]
    all_gather x1, waiting for transfers between devices: 152 us -> 144 us  [on_device(): token_segment = lax.all_gather(caches, 'req', axis=0, tiled=True)]
    all_to_all x0 -> x1, starting transfers between devices: none -> 5.83 us  [on_device(): gathered = jnp.concatenate(lax.all_to_all(repeated, 'col', 0, 0), axis=0)]
where the time goes in v1:
time: 303 us
  waiting for transfers between devices  196 us (65%)
  matrix products  74.5 us (25%)
  between operations  13.4 us (4%)
  other arithmetic  8.95 us (3%)
  starting transfers between devices  5.95 us (2%)
  local copies, waits for them, and re-layouts  3.95 us (1%)
    all_gather x1, waiting for transfers between devices, on_device(): token_segment = lax.all_gather(caches, 'req', axis=0, tiled=True)  144 us
    all_gather x1, waiting for transfers between devices, on_device(): lax.all_gather(feedforward_weight, 'col', axis=2, tiled=True)  36.4 us
    dot_general x1, matrix products, on_device(): jnp.einsum('sn,nhij->shij', select, token_segment, preferred_element_type...  32 us
    reduce_scatter x1, waiting for transfers between devices, on_device(): lax.psum_scatter(jnp.dot(head_out, head_output_weight, preferred_element_...  11.9 us
    dot_general x1, matrix products, on_device(): jnp.einsum('td,kdf->ktf', normed_two, token_segment[:2], preferred_elemen...  6.11 us
  transfers between devices with their start and end apart: 5, of which 4 were waited for; matrix products, arithmetic and copies ran while one was open for 11% of the time, Pallas kernels for 0%

profile of v1, /device:TPU:1, one launch (start us, length us, event | category | flops | bytes accessed | tf_op | source)
XLA Modules:
  0.0 302.5 jit_solution(2088774528153876671)
XLA Ops:
  8.0 1.2 fusion.38
  9.3 1.4 fusion.86
  10.6 1.2 fusion.50
  11.9 1.1 pad_maximum_fusion
  12.9 5.8 %all-to-all-start = ((bf16[2,256,1024]{2,1,0:T(8,128)(2,1)}), bf16[2,256,1024]{2,1,0:T(8,128)(2,1)}, u32[]{:S(2)}, u32[]{:S(2)}) async-start(bf16[2,256,1024]{2,1,0:T(8,128)(2,1)} %pad_maximum_fusion), calls=%async_computation | async-start | bytes 2097152 | tf_op jit(solution)/shard_map/all_to_all | solution.py:41
  18.9 1.7 all-to-all-done
  20.6 1.7 convolution_bitcast_fusion.1
  22.5 1.2 reduce-window.18
  24.7 4.2 %fusion.87 = (bf16[3,512,512]{1,2,0:T(8,128)(2,1)}, f32[3,512,512]{1,2,0:T(8,128)S(1)}) fusion(bf16[512,1024,1]{1,0,2:T(8,128)(2,1)} %bitcast.3, bf16[3,1024,512]{2,1,0:T(8,128)(2,1)S(1)} %copy-done), kind=kOutput, calls=%fused_computation.113 | convolution fusion | flops 1611399168 | bytes 8912896 | tf_op jit(solution)/shard_map/td,kdc->ktc/dot_general | solution.py:49
  31.1 2.4 convolution_convert_fusion
  34.6 3.9 %fusion.35 = bf16[6,1024,16]{1,0,2:T(8,128)(2,1)S(1)} fusion(bf16[64,1024,16]{1,2,0:T(8,128)(2,1)} %all-gather.4.cloned.1.call-done, s32[6]{0:T(128)S(1)} %bitcast.135), kind=kOutput, calls=%fused_computation.41 | convolution fusion | flops 12681600 | bytes 2293784 | tf_op jit(solution)/shard_map/sa,adr->sdr/dot_general | solution.py:55
  38.6 1.7 fusion.91
  42.0 4.8 %fusion.88 = (f32[4,512]{1,0:T(4,128)S(1)}, f32[4,512,512]{1,2,0:T(8,128)}) fusion(pred[512,512]{0,1:T(8,128)(4,1)S(1)} %fusion.46, bf16[512,4,128]{0,2,1:T(8,128)(2,1)S(1)} %add_convert_fusion, bf16[512,4,128]{0,2,1:T(8,128)(2,1)} %bitcast.128), kind=kOutput, calls=%fused_computation.114 | convolution fusion | flops 272630272 | bytes 5513216 | tf_op jit(solution)/shard_map/while/body/eval_jaxpr/sub | solution.py:104
  46.7 143.8 %all-gather.6.cloned.1.call-done = bf16[256,4,128,128]{3,2,1,0:T(8,128)(2,1)} async-done(((bf16[4,4,128,128]{3,2,1,0:T(8,128)(2,1)}), bf16[256,4,128,128]{3,2,1,0:T(8,128)(2,1)}) %all-gather.6.cloned.1.call-update) | async-done | bytes 33554448 | tf_op jit(solution)/shard_map/all_gather | solution.py:85
  190.6 32.0 %fusion.20 = bf16[6,4,128,128]{3,0,2,1:T(8,128)(2,1)S(1)} fusion(bf16[256,4,128,128]{3,2,1,0:T(8,128)(2,1)} %all-gather.6.cloned.1.call-done, s32[6]{0:T(128)S(1)} %bitcast.138), kind=kOutput, calls=%fused_computation.33 | convolution fusion | flops 201721344 | bytes 34340888 | tf_op jit(solution)/shard_map/sn,nhij->shij/dot_general | solution.py:88
  222.7 2.0 fusion.5
  224.7 4.1 %multiply_reduce_fusion.1 = (f32[512,4]{0,1:T(4,128)S(1)}, f32[512,4,128]{0,2,1:T(8,128)}) fusion(f32[512,4,128]{0,2,1:T(8,128)} %fusion.5, f32[512,4]{0,1:T(4,128)S(1)} %copy-done.9, bf16[512,4,128]{0,2,1:T(8,128)(2,1)S(1)} %bitcast.126, f32[4,512]{1,0:T(4,128)S(1)} %bitcast.132, pred[512,512]{0,1:T(8,128)(4,1)S(1)} %fusion.46, ...), kind=kOutput, calls=%fused_computation.53 | convolution fusion | flops 543160320 | bytes 3956736 | tf_op jit(solution)/shard_map/while/body/eval_jaxpr/hqk,khd->qhd/dot_general | solution.py:109
  228.8 3.1 %fusion.31 = bf16[512,4,128]{0,2,1:T(8,128)(2,1)S(1)} fusion(bf16[512,4,128]{0,2,1:T(8,128)(2,1)S(1)} %bitcast.127, f32[4,512,512]{1,2,0:T(8,128)} %get-tuple-element.44, f32[4,512]{1,0:T(4,128)S(1)} %get-tuple-element.42, f32[512,4,128]{0,2,1:T(8,128)} %get-tuple-element.46, f32[512,4]{0,1:T(4,128)S(1)} %add_rsqrt_fusion, f32[512,4]{0,1:T(4,128)S(1)} %copy-done.11), kind=kOutput, calls=%fused_computation.39 | convolution fusion | flops 271581184 | bytes 6316032 | tf_op jit(solution)/shard_map/while/body/eval_jaxpr/hqk,khd->qhd/dot_general | solution.py:106
  232.0 2.1 fusion.92
  234.7 11.9 %reduce-scatter.2.cloned.1.call-done = f32[256,1024]{1,0:T(8,128)} async-done(((f32[512,1024]{1,0:T(8,128)}), f32[256,1024]{1,0:T(8,128)}) %reduce-scatter.2.cloned.1.call-update) | async-done | bytes 1048592 | tf_op jit(solution)/shard_map/reduce_scatter | solution.py:117
  246.6 1.5 fusion.42
  248.1 36.4 %all-gather.8.cloned.1.call-done = bf16[3,1024,2816]{2,1,0:T(8,128)(2,1)} async-done(((bf16[3,1024,1408]{2,1,0:T(8,128)(2,1)}), bf16[3,1024,2816]{2,1,0:T(8,128)(2,1)}) %all-gather.8.cloned.1.call-update) | async-done | bytes 17301520 | tf_op jit(solution)/shard_map/all_gather | solution.py:125
  284.5 6.1 %fusion.7 = f32[2,256,2816]{2,1,0:T(8,128)S(1)} fusion(bf16[3,1024,2816]{2,1,0:T(8,128)(2,1)} %all-gather.8.cloned.1.call-done, bf16[256,1024]{1,0:T(8,128)(2,1)S(1)} %get-tuple-element.24, f32[1024]{0:T(1024)S(1)} %bitcast.133, f32[256]{0:T(256)S(1)} %add_rsqrt_fusion.1), kind=kOutput, calls=%fused_computation.10 | convolution fusion | flops 2953838592 | bytes 17830912 | tf_op jit(solution)/shard_map/td,kdf->ktf/dot_general | solution.py:126
  290.6 5.4 %fusion.32 = bf16[256,1024]{1,0:T(8,128)(2,1)} fusion(bf16[3,1024,2816]{2,1,0:T(8,128)(2,1)} %all-gather.8.cloned.1.call-done, f32[2,256,2816]{2,1,0:T(8,128)S(1)} %fusion.7, bf16[256,1024]{1,0:T(8,128)(2,1)} %copy-done.7), kind=kOutput, calls=%fused_computation.40 | convolution fusion | flops 1481506816 | bytes 12582912 | tf_op jit(solution)/shard_map/tf,df->td/dot_general | solution.py:130
  (72 shorter events, 8.4 us)
Async XLA Ops:
  6.5 18.2 %copy-start = (bf16[3,1024,512]{2,1,0:T(8,128)(2,1)S(1)}, bf16[3,1024,512]{2,1,0:T(8,128)(2,1)}, u32[]{:S(2)}) copy-start(bf16[3,1024,512]{2,1,0:T(8,128)(2,1)} %param.15) | copy-start | bytes 9437188
  6.5 12.2 %copy-start.16 = (s32[1,2,3]{2,1,0:T(2,128)S(1)}, s32[1,2,3]{2,1,0:T(2,128)}, u32[]{:S(2)}) copy-start(s32[1,2,3]{2,1,0:T(2,128)} %param.20) | copy-start | bytes 76
  6.5 14.1 %copy-start.8 = (bf16[2,1024,4]{1,2,0:T(4,128)(2,1)S(1)}, bf16[2,1024,4]{1,2,0:T(4,128)(2,1)}, u32[]{:S(2)}) copy-start(bf16[2,1024,4]{1,2,0:T(4,128)(2,1)} %param.16) | copy-start | bytes 49156
  6.5 15.8 %copy-start.14 = (f32[4]{0:T(128)S(1)}, f32[4]{0:T(128)}, u32[]{:S(2)}) copy-start(f32[4]{0:T(128)} %param.17) | copy-start | bytes 52
  6.5 28.1 %all-gather.4.cloned.1.call-start = ((), (), s32[]{:S(2)}) async-start(), calls=%async_computation.2 | async-start | bytes 3145728 | tf_op jit(solution)/shard_map/all_gather | solution.py:52
  7.3 183.3 %all-gather.6.cloned.1.call-start = ((), (), s32[]{:S(2)}) async-start(), calls=%async_computation.3 | async-start | bytes 34078720 | tf_op jit(solution)/shard_map/all_gather | solution.py:85
  12.9 7.7 %all-to-all-start = ((bf16[2,256,1024]{2,1,0:T(8,128)(2,1)}), bf16[2,256,1024]{2,1,0:T(8,128)(2,1)}, u32[]{:S(2)}, u32[]{:S(2)}) async-start(bf16[2,256,1024]{2,1,0:T(8,128)(2,1)} %pad_maximum_fusion), calls=%async_computation | async-start | bytes 2097152 | tf_op jit(solution)/shard_map/all_to_all | solution.py:41
  18.8 227.8 %reduce-scatter.2.cloned.1.call-start = ((), (), s32[]{:S(2)}) async-start(), calls=%async_computation.4 | async-start | bytes 3145728 | tf_op jit(solution)/shard_map/reduce_scatter | solution.py:117
  28.9 4.6 %copy-start.4 = (bf16[3,512,512]{1,2,0:T(8,128)(2,1)S(1)}, bf16[3,512,512]{1,2,0:T(8,128)(2,1)}, u32[]{:S(2)}) copy-start(bf16[3,512,512]{1,2,0:T(8,128)(2,1)} %get-tuple-element.29) | copy-start | bytes 4718596
  28.9 5.7 %copy-start.13 = (s32[1,6]{1,0:T(1,128)S(1)}, s32[1,6]{1,0:T(1,128)}, u32[]{:S(2)}) copy-start(s32[1,6]{1,0:T(1,128)} %param.21) | copy-start | bytes 76
  42.0 148.6 %copy-start.15 = (s32[1,6]{1,0:T(1,128)S(1)}, s32[1,6]{1,0:T(1,128)}, u32[]{:S(2)}) copy-start(s32[1,6]{1,0:T(1,128)} %param.22) | copy-start | bytes 76
  222.6 2.1 copy-start.5
  222.7 2.1 copy-start.6
  222.7 2.0 copy-start.9
  222.7 2.0 copy-start.10
  224.7 4.1 %copy-start.11 = (f32[512,4]{0,1:T(4,128)S(1)}, f32[512,4]{0,1:T(4,128)}, u32[]{:S(2)}) copy-start(f32[512,4]{0,1:T(4,128)} %fusion.68) | copy-start | bytes 24580
  228.8 3.1 %copy-start.3 = (bf16[512,1024]{1,0:T(8,128)(2,1)S(1)}, bf16[512,1024]{1,0:T(8,128)(2,1)}, u32[]{:S(2)}) copy-start(bf16[512,1024]{1,0:T(8,128)(2,1)} %param.24) | copy-start | bytes 3145732
  234.1 12.5 %copy-start.2 = (bf16[256,1024]{1,0:T(8,128)(2,1)S(1)}, bf16[256,1024]{1,0:T(8,128)(2,1)}, u32[]{:S(2)}) copy-start(bf16[256,1024]{1,0:T(8,128)(2,1)} %param.13) | copy-start | bytes 1572868
  234.1 50.4 %copy-start.12 = (f32[1,1024]{1,0:T(1,128)S(1)}, f32[1,1024]{1,0:T(1,128)}, u32[]{:S(2)}) copy-start(f32[1,1024]{1,0:T(1,128)} %get-tuple-element.27) | copy-start | bytes 12292
  234.1 50.4 %all-gather.8.cloned.1.call-start = ((), (), s32[]{:S(2)}) async-start(), calls=%async_computation.5 | async-start | bytes 25952256 | tf_op jit(solution)/shard_map/all_gather | solution.py:125
  248.0 36.4 %copy-start.7 = (bf16[256,1024]{1,0:T(8,128)(2,1)}, bf16[256,1024]{1,0:T(8,128)(2,1)S(1)}, u32[]{:S(2)}) copy-start(bf16[256,1024]{1,0:T(8,128)(2,1)S(1)} %get-tuple-element.24) | copy-start | bytes 1572868
  290.6 5.4 %copy-start.1 = (bf16[3,1024,512]{2,1,0:T(8,128)(2,1)S(1)}, bf16[3,1024,512]{2,1,0:T(8,128)(2,1)}, u32[]{:S(2)}) copy-start(bf16[3,1024,512]{2,1,0:T(8,128)(2,1)} %param.15) | copy-start | bytes 9437188
Sparse Core Ops, SparseCore 0:
  9.0 16.9 all-gather.3
  28.9 161.6 all-gather.5
  234.2 12.3 reduce-scatter.1
  248.2 36.2 all-gather.7
